TPU v7x, 128 devices: a whole 4x4x4 slice. The times are simulated.
128 devices in a mesh: seq: 4 (over x), exp: 32 (over y, z, core).
Axes of the slice: x: 4, y: 4, z: 4, core: 2. Of those that a mesh axis runs over, the one named last changes fastest.
Arguments:
- resid: bfloat16 [32, 384, 2048], P('exp', 'seq'), may hold values from -6 to 6
- qkv: bfloat16 [32, 384, 6144], P('exp', 'seq'), may hold values from -8 to 8
- w_out: bfloat16 [2048, 2048], P('seq'), may hold values from -0.125 to 0.125
- norm_gain: float32 [2048], replicated, may hold values from 0.1 to 1.9
- router_w: bfloat16 [2048, 64], replicated, may hold values from -0.125 to 0.125
- expert_ids: int32 [32, 384, 6], P('exp'), may hold values from 0 to 63, all different within a row; in each aligned block of 96 rows (0 to 95, 96 to 191, ..., all dimensions but the last counted through in order) at most 12 rows name the same one
- w_gate_up: bfloat16 [64, 2048, 2, 1408], P('exp', None, None, 'seq'), may hold values from -0.125 to 0.125
- w_down: bfloat16 [64, 1408, 2048], P('exp', 'seq'), may hold values from -0.15625 to 0.15625
Outputs:
- layer_out: bfloat16 [32, 384, 2048], P('exp', 'seq')
Inputs may be any that keep to these rules, and one draw needn't show every extreme that they name: `expert_ids`: each point names 6 different experts. In each aligned block of 96 points (the points of one device, in the order of sets and then points), no expert is named by more than 12 points, and in every draw some expert is named by exactly 12 points of some block.
All inputs are finite; a program needn't handle non-finite values.
Results may differ from a plain program's by a relative error of at most 0.0065.
Values may be sent and summed in bfloat16 or wider, within the bound.
No kernel may reach another device: no remote copies, remote signals or barrier semaphores. Data moves between devices by JAX's collectives and lax.ppermute only.
A program may use at most 128 MiB of HBM per device.

v0:
```python
import math
import jax
import jax.numpy as jnp
from jax import lax
from jax.sharding import PartitionSpec as P

H = 16
HD = 128
EXPERTS = 64
epsilon = 1e-05


def gate_weights(normed_rows, router_w, chosen):
    logits = jnp.dot(normed_rows, router_w, preferred_element_type=jnp.float32)
    match = chosen[:, :, None] == jnp.arange(logits.shape[1], dtype=jnp.int32)[None, None, :]
    picked = jnp.sum(jnp.where(match, logits[:, None, :], jnp.zeros((), logits.dtype)), axis=-1)
    squashed = jax.nn.sigmoid(picked)
    return squashed / jnp.sum(squashed, axis=-1, keepdims=True)


def slot_ranks(chosen, block_rows, experts):
    blocks = chosen.shape[0] // block_rows
    width = block_rows * chosen.shape[1]
    grouped = chosen.reshape(blocks, width)
    hits = (grouped[:, :, None] == jnp.arange(experts, dtype=jnp.int32)[None, None, :]).astype(
        jnp.bfloat16
    )
    lower = jnp.arange(width)[:, None] >= jnp.arange(width)[None, :]
    counts = jnp.einsum(
        "ij,bje->bie", lower.astype(jnp.bfloat16), hits, preferred_element_type=jnp.float32
    )
    ranks = jnp.sum(counts * hits.astype(jnp.float32), axis=-1) - 1
    return ranks.astype(jnp.int32).reshape(chosen.shape)


def expert_part(received, w_gate_up, w_down):
    both = jnp.einsum("aend,edgf->aengf", received, w_gate_up, preferred_element_type=jnp.float32)
    hidden = (jax.nn.silu(both[:, :, :, 0]) * both[:, :, :, 1]).astype(jnp.bfloat16)
    return jnp.einsum("aenf,efd->aend", hidden, w_down, preferred_element_type=jnp.float32)


def scatter_rows(normed_rows, slot_index, buffer_rows):
    slots = jnp.arange(buffer_rows, dtype=jnp.int32)
    select = jnp.sum((slot_index[None, :, :] == slots[:, None, None]).astype(jnp.bfloat16), axis=-1)
    return jnp.dot(select, normed_rows, preferred_element_type=jnp.float32).astype(jnp.bfloat16)


def combine_rows(out_table, slot_index, gate_vals):
    slots = jnp.arange(out_table.shape[0], dtype=jnp.int32)
    weights = jnp.sum(
        jnp.where(slot_index[:, :, None] == slots[None, None, :], gate_vals[:, :, None], 0.0),
        axis=1,
    )
    high = weights.astype(jnp.bfloat16)
    low = (weights - high.astype(jnp.float32)).astype(jnp.bfloat16)
    return jnp.dot(high, out_table, preferred_element_type=jnp.float32) + jnp.dot(
        low, out_table, preferred_element_type=jnp.float32
    )


def on_device(resid, qkv, w_out, norm_gain, router_w, expert_ids, w_gate_up, w_down):
    row_count = resid.shape[1]
    model_width = resid.shape[2]
    seq_size = lax.axis_size("seq")
    exp_size = lax.axis_size("exp")
    seq_length = row_count * seq_size
    head_local = H // seq_size
    local_width = head_local * HD
    packed = qkv.reshape(row_count, 3, seq_size, local_width)
    regrouped = lax.all_to_all(packed, "seq", split_axis=2, concat_axis=0, tiled=True)
    queries = regrouped[:, 0, 0].reshape(seq_length, head_local, HD)
    keys_all = regrouped[:, 1, 0].reshape(seq_length, head_local, HD)
    values_all = regrouped[:, 2, 0].reshape(seq_length, head_local, HD)
    query_block = min(seq_length, 512)

    def attend_block(query_rows):
        scores = jnp.einsum(
            "qhd,khd->hqk", query_rows, keys_all, preferred_element_type=jnp.float32
        ) / math.sqrt(HD)
        weights = jax.nn.softmax(scores, axis=-1).astype(jnp.bfloat16)
        mixed_heads = jnp.einsum(
            "hqk,khd->qhd", weights, values_all, preferred_element_type=jnp.float32
        )
        return mixed_heads.reshape(query_rows.shape[0], local_width).astype(jnp.bfloat16)

    attended = lax.map(
        attend_block, queries.reshape(seq_length // query_block, query_block, head_local, HD)
    )
    attended = attended.reshape(seq_length, local_width)
    back = lax.all_to_all(
        attended.reshape(seq_length, 1, local_width), "seq", split_axis=0, concat_axis=1, tiled=True
    )
    point_rows = back.reshape(row_count, model_width)
    projected = jnp.dot(
        point_rows,
        lax.all_gather(w_out, "seq", axis=0, tiled=True),
        preferred_element_type=jnp.float32,
    )
    mixed = resid[0].astype(jnp.float32) + projected
    meansq = jnp.mean(mixed * mixed, axis=-1, keepdims=True)
    normed = (mixed * lax.rsqrt(meansq + epsilon) * norm_gain).astype(jnp.bfloat16)
    exp_local = w_gate_up.shape[0]
    slot_cap = row_count // 8
    gathered = lax.all_gather(normed, "seq", axis=0, tiled=True)
    chosen = expert_ids[0]
    gate_vals = gate_weights(gathered, router_w, chosen)
    ranks = slot_ranks(chosen, row_count, EXPERTS)
    owner_rows = seq_size * slot_cap
    source_block = (jnp.arange(seq_length, dtype=jnp.int32) // row_count)[:, None]
    slot_index = chosen * owner_rows + source_block * slot_cap + ranks
    outgoing = scatter_rows(gathered, slot_index, EXPERTS * owner_rows)
    outgoing = outgoing.reshape(exp_size, exp_local, owner_rows, model_width)
    partial_out = expert_part(
        lax.all_to_all(outgoing, "exp", split_axis=0, concat_axis=0, tiled=True), w_gate_up, w_down
    ).astype(jnp.bfloat16)
    returned = lax.all_to_all(partial_out, "exp", split_axis=0, concat_axis=0, tiled=True)
    out_table = returned.reshape(-1, model_width)
    expert_sum = lax.psum_scatter(
        combine_rows(out_table, slot_index, gate_vals).astype(jnp.bfloat16),
        "seq",
        scatter_dimension=0,
        tiled=True,
    ).astype(jnp.float32)
    return (mixed + expert_sum).astype(jnp.bfloat16).reshape(1, row_count, model_width)


def solution(mesh):
    in_specs = (
        P("exp", "seq", None),
        P("exp", "seq", None),
        P("seq", None),
        P(),
        P(),
        P("exp", None, None),
        P("exp", None, None, "seq"),
        P("exp", "seq", None),
    )
    out_specs = P("exp", "seq", None)
    return jax.shard_map(
        on_device, mesh=mesh, in_specs=in_specs, out_specs=out_specs, check_vma=False
    )
```

profile of v0, /device:TPU:0, one launch (start us, length us, event | category | flops | bytes accessed | tf_op | source)
XLA Modules:
  0.0 582.8 jit_solution(9345225432618470734)
XLA Ops:
  6.5 0.7 all-gather.3.cloned.1.call-update
  7.3 2.9 reshape.139
  10.2 1.5 copy.111
  11.7 27.4 %all_to_all.43 = bf16[96,3,4,512]{3,0,1,2:T(8,128)(2,1)S(1)} all-to-all(bf16[96,3,4,512]{3,0,1,2:T(8,128)(2,1)S(1)} %copy.111), channel_id=1, replica_groups=mesh['seq'=4,'exp'=32] {'seq'}, dimensions={2} | all-to-all | bytes 2359296 | tf_op jit(solution)/shard_map/all_to_all | solution.py:70
  39.2 0.1 copy.112
  39.2 1.0 fusion.48
  40.2 1.9 copy.117
  42.2 1.9 copy.113
  44.1 0.9 copy.114
  45.0 3.5 fusion.49
  48.5 2.2 convolution_convert_fusion.1
  50.7 0.5 broadcast.124
  51.2 1.5 reduce.1
  52.7 1.2 copy.150
  53.9 1.0 reshape.149
  54.9 15.5 %all_to_all.44 = bf16[4,2,24576]{2,1,0:T(2,128)(2,1)S(1)} all-to-all(bf16[4,2,24576]{2,1,0:T(2,128)(2,1)} %reshape.149), channel_id=1, replica_groups=mesh['seq'=4,'exp'=32] {'seq'}, dimensions={0} | all-to-all | bytes 786432 | tf_op jit(solution)/shard_map/all_to_all | solution.py:90
  70.4 1.7 reshape.150
  72.1 1.2 copy.138
  73.3 0.3 copy.120
  73.7 30.5 %all-gather.3.cloned.1.call-done = bf16[2048,2048]{1,0:T(8,128)(2,1)} async-done(((bf16[512,2048]{1,0:T(8,128)(2,1)}), bf16[2048,2048]{1,0:T(8,128)(2,1)}) %all-gather.3.cloned.1.call-update) | async-done | bytes 8388624 | tf_op jit(solution)/shard_map/all_gather | solution.py:96
  104.1 5.0 multiply_reduce_fusion.1
  109.2 0.9 copy-done.2
  110.1 0.9 multiply_convert_fusion
  111.0 0.1 copy.121
  111.2 0.2 eq.56
  111.3 0.5 fusion.28
  111.8 0.2 convert_element_type.105
  112.0 0.1 copy.125
  112.2 5.6 fusion.2
  117.8 20.6 %all-gather.5.cloned.1.call-done = bf16[384,2048]{1,0:T(8,128)(2,1)} async-done(((bf16[96,2048]{1,0:T(8,128)(2,1)}), bf16[384,2048]{1,0:T(8,128)(2,1)}) %all-gather.5.cloned.1.call-update) | async-done | bytes 1572880 | tf_op jit(solution)/shard_map/all_gather | solution.py:104
  138.4 8.7 %convolution_convert_fusion = bf16[3072,2048]{1,0:T(8,128)(2,1)S(1)} fusion(bf16[3072,384]{1,0:T(8,128)(2,1)} %fusion.2, bf16[384,2048]{1,0:T(8,128)(2,1)} %all-gather.5.cloned.1.call-done), kind=kOutput, calls=%fused_computation.9 | convolution fusion | flops 4838129664 | bytes 16515072 | tf_op jit(solution)/shard_map/dot_general | solution.py:45
  147.1 147.5 %all_to_all.45 = bf16[32,2,48,2048]{3,2,1,0:T(8,128)(2,1)} all-to-all(bf16[32,2,48,2048]{3,2,1,0:T(8,128)(2,1)S(1)} %bitcast.99), channel_id=1, replica_groups=mesh['seq'=4,'exp'=32] {'exp'}, dimensions={0} | all-to-all | bytes 25165824 | tf_op jit(solution)/shard_map/all_to_all | solution.py:114
  294.6 16.0 %fusion.8 = f32[32,2,48,2,352]{4,2,3,0,1:T(8,128)} fusion(bf16[2,2048,2,352]{1,3,2,0:T(8,128)(2,1)} %param.14, bf16[32,2,48,2048]{3,2,1,0:T(8,128)(2,1)} %all_to_all.45), kind=kOutput, calls=%fused_computation.16 | convolution fusion | flops 8858370048 | bytes 27000832 | tf_op jit(solution)/shard_map/aend,edgf->aengf/dot_general | solution.py:37
  310.6 10.7 %convert_bitcast_fusion = bf16[32,2,48,2048]{3,2,0,1:T(8,128)(2,1)S(1)} fusion(bf16[2,352,2048]{2,1,0:T(8,128)(2,1)S(1)} %copy-done, f32[32,2,48,2,352]{4,2,3,0,1:T(8,128)} %fusion.8), kind=kOutput, calls=%fused_computation.8 | convolution fusion | flops 4441964544 | bytes 24117248 | tf_op jit(solution)/shard_map/aenf,efd->aend/dot_general | solution.py:39
  321.3 5.2 copy.128
  326.5 5.2 all-to-all-start.3
  331.7 0.3 reduce-scatter.2.cloned.1.call-start
  332.0 0.2 convert_element_type.102
  332.2 0.1 fusion.41
  332.3 0.1 copy.123
  332.4 0.6 fusion.50
  333.0 0.1 select_reduce_fusion.1
  333.2 8.6 %select_reduce_fusion = f32[384,3072]{1,0:T(8,128)} fusion(f32[384,6]{0,1:T(8,128)S(1)} %multiply_divide_fusion, s32[384,6]{0,1:T(8,128)S(1)} %copy.123), kind=kLoop, calls=%fused_computation.2 | loop fusion | flops 20054016 | bytes 4737024 | tf_op jit(solution)/shard_map/reduce_sum | solution.py:50
  341.7 167.1 %all-to-all-done.3 = bf16[32,2,48,2048]{3,2,1,0:T(8,128)(2,1)} async-done(((bf16[32,2,48,2048]{3,2,1,0:T(8,128)(2,1)}), bf16[32,2,48,2048]{3,2,1,0:T(8,128)(2,1)}, u32[]{:S(2)}, u32[]{:S(2)}) %all-to-all-start.3) | async-done | bytes 12582944 | tf_op jit(solution)/shard_map/all_to_all | solution.py:116
  508.9 11.0 %fusion.32 = f32[384,2048]{1,0:T(8,128)S(1)} fusion(bf16[3072,2048]{1,0:T(8,128)(2,1)} %bitcast.26, f32[384,3072]{1,0:T(8,128)} %select_reduce_fusion), kind=kOutput, calls=%fused_computation.33 | convolution fusion | flops 4833017856 | bytes 20447232 | tf_op jit(solution)/shard_map/dot_general | solution.py:56
  519.9 9.8 %add_convert_fusion = bf16[384,2048]{1,0:T(8,128)(2,1)} fusion(f32[384,2048]{1,0:T(8,128)S(1)} %fusion.32, bf16[3072,2048]{1,0:T(8,128)(2,1)} %bitcast.26, f32[384,3072]{1,0:T(8,128)S(1)} %copy-done.3), kind=kOutput, calls=%fused_computation.17 | convolution fusion | flops 4838129664 | bytes 22020096 | tf_op jit(solution)/shard_map/dot_general | solution.py:56
  529.7 44.4 %reduce-scatter.2.cloned.1.call-done = bf16[96,2048]{1,0:T(8,128)(2,1)} async-done(((bf16[384,2048]{1,0:T(8,128)(2,1)}), bf16[96,2048]{1,0:T(8,128)(2,1)}) %reduce-scatter.2.cloned.1.call-update) | async-done | bytes 393232 | tf_op jit(solution)/shard_map/reduce_scatter | solution.py:118
  574.2 2.1 fusion.36
  (28 shorter events, 0.3 us)
Async XLA Ops:
  6.5 304.1 %copy-start = (bf16[2,352,2048]{2,1,0:T(8,128)(2,1)S(1)}, bf16[2,352,2048]{2,1,0:T(8,128)(2,1)}, u32[]{:S(2)}) copy-start(bf16[2,352,2048]{2,1,0:T(8,128)(2,1)} %param.15) | copy-start | bytes 8650756
  6.5 97.6 %all-gather.3.cloned.1.call-start = ((), (), s32[]{:S(2)}) async-start(), calls=%async_computation.5 | async-start | bytes 10485760 | tf_op jit(solution)/shard_map/all_gather | solution.py:96
  7.3 131.1 %all-gather.5.cloned.1.call-start = ((), (), s32[]{:S(2)}) async-start(), calls=%async_computation.6 | async-start | bytes 1966080 | tf_op jit(solution)/shard_map/all_gather | solution.py:104
  104.1 6.0 %copy-start.7 = (f32[2048]{0:T(1024)S(1)}, f32[2048]{0:T(1024)}, u32[]{:S(2)}) copy-start(f32[2048]{0:T(1024)} %param.11) | copy-start | bytes 24580
  104.1 6.9 %copy-start.6 = (s32[1,384,6]{1,0,2:T(1,128)S(1)}, s32[1,384,6]{1,0,2:T(1,128)}, u32[]{:S(2)}) copy-start(s32[1,384,6]{1,0,2:T(1,128)} %param.13) | copy-start | bytes 27652
  109.1 1.0 copy-start.2
  326.5 5.9 %copy-start.4 = (bf16[384,2048]{1,0:T(8,128)(2,1)S(1)}, bf16[384,2048]{1,0:T(8,128)(2,1)}, u32[]{:S(2)}) copy-start(bf16[384,2048]{1,0:T(8,128)(2,1)} %all-gather.5.cloned.1.call-done) | copy-start | bytes 4718596
  326.5 5.9 %copy-start.5 = (bf16[2048,64]{0,1:T(8,128)(2,1)S(1)}, bf16[2048,64]{0,1:T(8,128)(2,1)}, u32[]{:S(2)}) copy-start(bf16[2048,64]{0,1:T(8,128)(2,1)} %param.12) | copy-start | bytes 786436
  326.5 182.3 %all-to-all-start.3 = ((bf16[32,2,48,2048]{3,2,1,0:T(8,128)(2,1)}), bf16[32,2,48,2048]{3,2,1,0:T(8,128)(2,1)}, u32[]{:S(2)}, u32[]{:S(2)}) async-start(bf16[32,2,48,2048]{3,2,1,0:T(8,128)(2,1)} %copy.128), calls=%async_computation.3 | async-start | bytes 25165824 | tf_op jit(solution)/shard_map/all_to_all | solution.py:116
  331.7 242.5 %reduce-scatter.2.cloned.1.call-start = ((), (), s32[]{:S(2)}) async-start(), calls=%async_computation.7 | async-start | bytes 1966080 | tf_op jit(solution)/shard_map/reduce_scatter | solution.py:118
  508.9 11.0 %copy-start.3 = (f32[384,3072]{1,0:T(8,128)S(1)}, f32[384,3072]{1,0:T(8,128)}, u32[]{:S(2)}) copy-start(f32[384,3072]{1,0:T(8,128)} %select_reduce_fusion) | copy-start | bytes 14155780
  519.9 56.3 %copy-start.1 = (bf16[2,352,2048]{2,1,0:T(8,128)(2,1)S(1)}, bf16[2,352,2048]{2,1,0:T(8,128)(2,1)}, u32[]{:S(2)}) copy-start(bf16[2,352,2048]{2,1,0:T(8,128)(2,1)} %param.15) | copy-start | bytes 8650756
Sparse Core Ops, SparseCore 0:
  9.0 95.0 all-gather.2
  111.1 27.2 all-gather.4
  529.9 44.2 reduce-scatter.1
where the time goes:
time: 583 us
  waiting for transfers between devices  263 us (45%)
  blocking collectives  190 us (33%)
  matrix products  68 us (12%)
  local copies, waits for them, and re-layouts  23.2 us (4%)
  other arithmetic  18.9 us (3%)
  between operations  13.3 us (2%)
    all_to_all x1, waiting for transfers between devices, on_device(): lax.all_to_all(partial_out, 'exp', split_axis=0, concat_axis=0, tiled=True)  167 us
    all_to_all x1, blocking collectives, on_device(): lax.all_to_all(outgoing, 'exp', split_axis=0, concat_axis=0, tiled=True)  148 us
    reduce_scatter x1, waiting for transfers between devices, on_device(): lax.psum_scatter(combine_rows(out_table, slot_index, gate_vals).astype(jn...  44.4 us
    all_gather x1, waiting for transfers between devices, on_device(): lax.all_gather(w_out, 'seq', axis=0, tiled=True)  30.5 us
    all_to_all x1, blocking collectives, on_device(): lax.all_to_all(packed, 'seq', split_axis=2, concat_axis=0, tiled=True)  27.4 us
    all_gather x1, waiting for transfers between devices, on_device(): gathered = lax.all_gather(normed, 'seq', axis=0, tiled=True)  20.6 us
    dot_general x1, matrix products, expert_part(): jnp.einsum('aend,edgf->aengf', received, w_gate_up, preferred_element_typ...  16 us
    all_to_all x1, blocking collectives, on_device(): lax.all_to_all(attended.reshape(seq_length, 1, local_width), 'seq', split...  15.5 us
  transfers between devices with their start and end apart: 4, of which 4 were waited for; matrix products, arithmetic and copies ran while one was open for 7% of the time, Pallas kernels for 0%

commit v1 on v0

--- a/solution.py
+++ b/solution.py
@@ -8,6 +8,11 @@
 HD = 128
 EXPERTS = 64
 epsilon = 1e-05
+
+
+def swapped_in(block, axis, along):
+    repeated = jnp.stack([block] * lax.axis_size(axis))
+    return jnp.concatenate(lax.all_to_all(repeated, axis, 0, 0), axis=along)
 
 
 def gate_weights(normed_rows, router_w, chosen):
@@ -91,11 +96,7 @@
         attended.reshape(seq_length, 1, local_width), "seq", split_axis=0, concat_axis=1, tiled=True
     )
     point_rows = back.reshape(row_count, model_width)
-    projected = jnp.dot(
-        point_rows,
-        lax.all_gather(w_out, "seq", axis=0, tiled=True),
-        preferred_element_type=jnp.float32,
-    )
+    projected = jnp.dot(point_rows, swapped_in(w_out, "seq", 0), preferred_element_type=jnp.float32)
     mixed = resid[0].astype(jnp.float32) + projected
     meansq = jnp.mean(mixed * mixed, axis=-1, keepdims=True)
     normed = (mixed * lax.rsqrt(meansq + epsilon) * norm_gain).astype(jnp.bfloat16)

time: 583 us -> 641 us (1.099)
  waiting for transfers between devices: 263 us -> 320 us
  blocking collectives: 190 us -> 179 us
    all_to_all x0 -> x1, waiting for transfers between devices: none -> 88.3 us  [swapped_in(): return jnp.concatenate(lax.all_to_all(repeated, axis, 0, 0), axis=along)]
    all_gather x1 -> x0, waiting for transfers between devices: 30.5 us -> none  [on_device(): lax.all_gather(w_out, 'seq', axis=0, tiled=True)]
    all_to_all x1, blocking collectives: 27.4 us -> 20.7 us  [on_device(): lax.all_to_all(packed, 'seq', split_axis=2, concat_axis=0, tiled=True)]
  transfers between devices with their start and end apart: 4 -> 4, of which waited for: 4 -> 4; matrix products, arithmetic and copies ran while one was open for 7% -> 3% of each run, Pallas kernels for 0% -> 0%
where the time goes in v1:
time: 641 us; the launch traced here: 640 us
  waiting for transfers between devices  320 us (50%)
  blocking collectives  179 us (28%)
  matrix products  68 us (11%)
  local copies, waits for them, and re-layouts  29.1 us (5%)
  other arithmetic  19 us (3%)
  between operations  13.6 us (2%)
  starting transfers between devices  11.4 us (2%)
    all_to_all x1, waiting for transfers between devices, on_device(): lax.all_to_all(partial_out, 'exp', split_axis=0, concat_axis=0, tiled=True)  167 us
    all_to_all x1, blocking collectives, on_device(): lax.all_to_all(outgoing, 'exp', split_axis=0, concat_axis=0, tiled=True)  148 us
    all_to_all x1, waiting for transfers between devices, swapped_in(): return jnp.concatenate(lax.all_to_all(repeated, axis, 0, 0), axis=along)  88.3 us
    reduce_scatter x1, waiting for transfers between devices, on_device(): lax.psum_scatter(combine_rows(out_table, slot_index, gate_vals).astype(jn...  44.4 us
    all_to_all x1, blocking collectives, on_device(): lax.all_to_all(packed, 'seq', split_axis=2, concat_axis=0, tiled=True)  20.7 us
    all_gather x1, waiting for transfers between devices, on_device(): gathered = lax.all_gather(normed, 'seq', axis=0, tiled=True)  20.3 us
    dot_general x1, matrix products, expert_part(): jnp.einsum('aend,edgf->aengf', received, w_gate_up, preferred_element_typ...  16 us
  transfers between devices with their start and end apart: 4, of which 4 were waited for; matrix products, arithmetic and copies ran while one was open for 3% of the time, Pallas kernels for 0%

profile of v1, /device:TPU:0, one launch (start us, length us, event | category | flops | bytes accessed | tf_op | source)
XLA Modules:
  0.0 640.3 jit_solution(17354034315942806847)
XLA Ops:
  6.5 2.9 reshape.144
  9.5 1.5 copy.111
  11.0 20.7 %all_to_all.48 = bf16[96,3,4,512]{3,0,1,2:T(8,128)(2,1)S(1)} all-to-all(bf16[96,3,4,512]{3,0,1,2:T(8,128)(2,1)S(1)} %copy.111), channel_id=1, replica_groups=mesh['seq'=4,'exp'=32] {'seq'}, dimensions={2} | all-to-all | bytes 2359296 | tf_op jit(solution)/shard_map/all_to_all | solution.py:75
  31.8 0.9 fusion.48
  32.7 1.9 copy.117
  34.6 1.9 copy.113
  36.5 0.9 copy.114
  37.5 3.4 fusion.49
  40.8 2.2 convolution_convert_fusion.1
  43.1 0.6 broadcast.126
  43.7 1.6 reduce.1
  45.3 1.2 copy.150
  46.5 1.0 reshape.155
  47.5 10.8 %all_to_all.49 = bf16[4,2,24576]{2,1,0:T(2,128)(2,1)S(1)} all-to-all(bf16[4,2,24576]{2,1,0:T(2,128)(2,1)} %reshape.155), channel_id=1, replica_groups=mesh['seq'=4,'exp'=32] {'seq'}, dimensions={0} | all-to-all | bytes 786432 | tf_op jit(solution)/shard_map/all_to_all | solution.py:95
  58.3 5.9 stack.2
  64.2 5.7 all-to-all-start.2
  69.9 0.2 all-gather.2.cloned.1.call-start
  70.1 1.7 reshape.156
  71.7 1.2 copy.138
  72.9 0.3 copy.120
  73.3 88.3 %all-to-all-done.2 = bf16[4,512,2048]{2,1,0:T(8,128)(2,1)} async-done(((bf16[4,512,2048]{2,1,0:T(8,128)(2,1)}), bf16[4,512,2048]{2,1,0:T(8,128)(2,1)}, u32[]{:S(2)}, u32[]{:S(2)}) %all-to-all-start.2) | async-done | bytes 8388640 | tf_op jit(solution)/shard_map/all_to_all | solution.py:15
  161.7 5.0 multiply_reduce_fusion.1
  166.7 0.9 copy-done.2
  167.6 0.9 multiply_convert_fusion
  168.5 0.1 copy.121
  168.7 0.2 eq.56
  168.8 0.5 fusion.28
  169.3 0.2 convert_element_type.105
  169.5 0.1 copy.125
  169.7 5.6 fusion.2
  175.3 20.3 %all-gather.2.cloned.1.call-done = bf16[384,2048]{1,0:T(8,128)(2,1)} async-done(((bf16[96,2048]{1,0:T(8,128)(2,1)}), bf16[384,2048]{1,0:T(8,128)(2,1)}) %all-gather.2.cloned.1.call-update) | async-done | bytes 1572880 | tf_op jit(solution)/shard_map/all_gather | solution.py:105
  195.6 8.7 %convolution_convert_fusion = bf16[3072,2048]{1,0:T(8,128)(2,1)S(1)} fusion(bf16[3072,384]{1,0:T(8,128)(2,1)} %fusion.2, bf16[384,2048]{1,0:T(8,128)(2,1)} %all-gather.2.cloned.1.call-done), kind=kOutput, calls=%fused_computation.9 | convolution fusion | flops 4838129664 | bytes 16515072 | tf_op jit(solution)/shard_map/dot_general | solution.py:50
  204.3 147.5 %all_to_all.50 = bf16[32,2,48,2048]{3,2,1,0:T(8,128)(2,1)} all-to-all(bf16[32,2,48,2048]{3,2,1,0:T(8,128)(2,1)S(1)} %bitcast.100), channel_id=1, replica_groups=mesh['seq'=4,'exp'=32] {'exp'}, dimensions={0} | all-to-all | bytes 25165824 | tf_op jit(solution)/shard_map/all_to_all | solution.py:115
  351.8 16.0 %fusion.8 = f32[32,2,48,2,352]{4,2,3,0,1:T(8,128)} fusion(bf16[2,2048,2,352]{1,3,2,0:T(8,128)(2,1)} %param.14, bf16[32,2,48,2048]{3,2,1,0:T(8,128)(2,1)} %all_to_all.50), kind=kOutput, calls=%fused_computation.16 | convolution fusion | flops 8858370048 | bytes 27000832 | tf_op jit(solution)/shard_map/aend,edgf->aengf/dot_general | solution.py:42
  367.8 10.7 %convert_bitcast_fusion = bf16[32,2,48,2048]{3,2,0,1:T(8,128)(2,1)S(1)} fusion(bf16[2,352,2048]{2,1,0:T(8,128)(2,1)S(1)} %copy-done, f32[32,2,48,2,352]{4,2,3,0,1:T(8,128)} %fusion.8), kind=kOutput, calls=%fused_computation.8 | convolution fusion | flops 4441964544 | bytes 24117248 | tf_op jit(solution)/shard_map/aenf,efd->aend/dot_general | solution.py:44
  378.6 5.2 copy.128
  383.8 5.2 all-to-all-start.4
  389.0 0.3 reduce-scatter.2.cloned.1.call-start
  389.3 0.2 convert_element_type.102
  389.5 0.1 fusion.41
  389.6 0.1 copy.123
  389.7 0.6 fusion.50
  390.4 8.6 %select_reduce_fusion = f32[384,3072]{1,0:T(8,128)} fusion(f32[384,6]{0,1:T(8,128)S(1)} %multiply_divide_fusion, s32[384,6]{0,1:T(8,128)S(1)} %copy.123), kind=kLoop, calls=%fused_computation.2 | loop fusion | flops 20054016 | bytes 4737024 | tf_op jit(solution)/shard_map/reduce_sum | solution.py:55
  399.0 167.1 %all-to-all-done.4 = bf16[32,2,48,2048]{3,2,1,0:T(8,128)(2,1)} async-done(((bf16[32,2,48,2048]{3,2,1,0:T(8,128)(2,1)}), bf16[32,2,48,2048]{3,2,1,0:T(8,128)(2,1)}, u32[]{:S(2)}, u32[]{:S(2)}) %all-to-all-start.4) | async-done | bytes 12582944 | tf_op jit(solution)/shard_map/all_to_all | solution.py:117
  566.1 11.0 %fusion.32 = f32[384,2048]{1,0:T(8,128)S(1)} fusion(bf16[3072,2048]{1,0:T(8,128)(2,1)} %bitcast.27, f32[384,3072]{1,0:T(8,128)} %select_reduce_fusion), kind=kOutput, calls=%fused_computation.33 | convolution fusion | flops 4833017856 | bytes 20447232 | tf_op jit(solution)/shard_map/dot_general | solution.py:61
  577.2 9.8 %add_convert_fusion = bf16[384,2048]{1,0:T(8,128)(2,1)} fusion(f32[384,2048]{1,0:T(8,128)S(1)} %fusion.32, bf16[3072,2048]{1,0:T(8,128)(2,1)} %bitcast.27, f32[384,3072]{1,0:T(8,128)S(1)} %copy-done.3), kind=kOutput, calls=%fused_computation.17 | convolution fusion | flops 4838129664 | bytes 22020096 | tf_op jit(solution)/shard_map/dot_general | solution.py:61
  587.0 44.4 %reduce-scatter.2.cloned.1.call-done = bf16[96,2048]{1,0:T(8,128)(2,1)} async-done(((bf16[384,2048]{1,0:T(8,128)(2,1)}), bf16[96,2048]{1,0:T(8,128)(2,1)}) %reduce-scatter.2.cloned.1.call-update) | async-done | bytes 393232 | tf_op jit(solution)/shard_map/reduce_scatter | solution.py:119
  631.4 2.1 fusion.36
  (28 shorter events, 0.4 us)
Async XLA Ops:
  6.5 361.3 %copy-start = (bf16[2,352,2048]{2,1,0:T(8,128)(2,1)S(1)}, bf16[2,352,2048]{2,1,0:T(8,128)(2,1)}, u32[]{:S(2)}) copy-start(bf16[2,352,2048]{2,1,0:T(8,128)(2,1)} %param.15) | copy-start | bytes 8650756
  64.2 97.5 %all-to-all-start.2 = ((bf16[4,512,2048]{2,1,0:T(8,128)(2,1)}), bf16[4,512,2048]{2,1,0:T(8,128)(2,1)}, u32[]{:S(2)}, u32[]{:S(2)}) async-start(bf16[4,512,2048]{2,1,0:T(8,128)(2,1)} %stack.2), calls=%async_computation.2 | async-start | bytes 16777216 | tf_op jit(solution)/shard_map/all_to_all | solution.py:15
  69.9 125.8 %all-gather.2.cloned.1.call-start = ((), (), s32[]{:S(2)}) async-start(), calls=%async_computation.6 | async-start | bytes 1966080 | tf_op jit(solution)/shard_map/all_gather | solution.py:105
  161.7 6.0 copy-start.7
  161.7 6.9 %copy-start.6 = (s32[1,384,6]{1,0,2:T(1,128)S(1)}, s32[1,384,6]{1,0,2:T(1,128)}, u32[]{:S(2)}) copy-start(s32[1,384,6]{1,0,2:T(1,128)} %param.13) | copy-start | bytes 27652
  166.7 0.9 copy-start.2
  383.8 5.9 copy-start.4
  383.8 5.9 copy-start.5
  383.8 182.3 %all-to-all-start.4 = ((bf16[32,2,48,2048]{3,2,1,0:T(8,128)(2,1)}), bf16[32,2,48,2048]{3,2,1,0:T(8,128)(2,1)}, u32[]{:S(2)}, u32[]{:S(2)}) async-start(bf16[32,2,48,2048]{3,2,1,0:T(8,128)(2,1)} %copy.128), calls=%async_computation.4 | async-start | bytes 25165824 | tf_op jit(solution)/shard_map/all_to_all | solution.py:117
  389.0 242.5 %reduce-scatter.2.cloned.1.call-start = ((), (), s32[]{:S(2)}) async-start(), calls=%async_computation.7 | async-start | bytes 1966080 | tf_op jit(solution)/shard_map/reduce_scatter | solution.py:119
  566.1 11.0 %copy-start.3 = (f32[384,3072]{1,0:T(8,128)S(1)}, f32[384,3072]{1,0:T(8,128)}, u32[]{:S(2)}) copy-start(f32[384,3072]{1,0:T(8,128)} %select_reduce_fusion) | copy-start | bytes 14155780
  577.2 56.3 %copy-start.1 = (bf16[2,352,2048]{2,1,0:T(8,128)(2,1)S(1)}, bf16[2,352,2048]{2,1,0:T(8,128)(2,1)}, u32[]{:S(2)}) copy-start(bf16[2,352,2048]{2,1,0:T(8,128)(2,1)} %param.15) | copy-start | bytes 8650756
Sparse Core Ops, SparseCore 0:
  168.6 26.9 all-gather.1
  587.1 44.2 reduce-scatter.1
